TPU v7x, 256 devices: a whole 4x4x8 slice. The times are simulated.
256 devices in a mesh: blk: 64 (over z, x, core), req: 4 (over y).
Axes of the slice: x: 4, y: 4, z: 8, core: 2. Of those that a mesh axis runs over, the one named last changes fastest.
Arguments:
- tokens: bfloat16 [32, 4, 2048], P('req'), may hold values from -6 to 6
- lengths: int32 [32], replicated, may hold values from 1 to 8192, 104857 in all
- slot_request: int32 [32], replicated, may hold values from 0 to 31, each once
- ln1_gain: float32 [2048], replicated, may hold values from 0.5 to 1.5
- ln1_bias: float32 [2048], replicated, may hold values from -3 to 3
- w_query: bfloat16 [2048, 2048], P(None, 'blk'), may hold values from -0.125 to 0.125
- w_key: bfloat16 [2048, 2048], P(None, 'blk'), may hold values from -0.125 to 0.125
- w_value: bfloat16 [2048, 2048], P(None, 'blk'), may hold values from -0.125 to 0.125
- b_query: float32 [2048], P('blk'), may hold values from -3 to 3
- b_key: float32 [2048], P('blk'), may hold values from -3 to 3
- b_value: float32 [2048], P('blk'), may hold values from -3 to 3
- cache_keys: bfloat16 [32, 8192, 2048], P('req', 'blk'), may hold values from -500 to 500
- cache_values: bfloat16 [32, 8192, 2048], P('req', 'blk'), may hold values from -9 to 9
- w_out: bfloat16 [2048, 2048], P(None, 'blk'), may hold values from -0.125 to 0.125
- ln2_gain: float32 [2048], replicated, may hold values from 0.5 to 1.5
- ln2_bias: float32 [2048], replicated, may hold values from -3 to 3
- w_gate: bfloat16 [2048, 5632], P(None, 'blk'), may hold values from -0.125 to 0.125
- w_up: bfloat16 [2048, 5632], P(None, 'blk'), may hold values from -0.125 to 0.125
- w_down: bfloat16 [5632, 2048], P('blk'), may hold values from -0.078125 to 0.078125
Outputs:
- layer_out: bfloat16 [32, 4, 2048], P('req', None, 'blk')
- new_keys: bfloat16 [32, 4, 2048], P('req', None, 'blk')
- new_values: bfloat16 [32, 4, 2048], P('req', None, 'blk')
Inputs may be any that keep to these rules, and one draw needn't show every extreme that they name: `lengths`: every request has 1 or more cached tokens; some request has exactly 8192. A permutation of the 32 requests: cache slot i holds request slot_request[i].
All inputs are finite; a program needn't handle non-finite values.
Results may differ from a plain program's by a relative error of at most 0.012.
The roundings to bfloat16 on the way count: a program that leaves them out, or rounds other values in their place, can miss the bound.
Values may be sent and summed in bfloat16 or wider, within the bound.
No kernel may reach another device: no remote copies, remote signals or barrier semaphores. Data moves between devices by JAX's collectives and lax.ppermute only.
A program may use at most 192 MiB of HBM per device.

v0:
```python
import jax
import jax.numpy as jnp
from jax import lax
from jax.sharding import PartitionSpec as P

D = 2048
HEADS = 32
HEAD_DIM = 64
ROT = 16
NEW = 4


def layer_norm(values, norm_gain, norm_bias):
    average = jnp.mean(values, -1, keepdims=True)
    centered = values - average
    variance = jnp.mean(centered * centered, -1, keepdims=True)
    return centered * lax.rsqrt(variance + 1e-05) * norm_gain + norm_bias


def rotate(heads, positions):
    half_rot = ROT // 2
    frequency = 10000.0 ** (-2.0 * jnp.arange(half_rot, dtype=jnp.float32) / ROT)
    angles = positions.astype(jnp.float32)[..., None, None] * frequency
    cosine = jnp.cos(angles)
    sine = jnp.sin(angles)
    leading = heads[..., :half_rot]
    second = heads[..., half_rot:ROT]
    unrotated = heads[..., ROT:]
    return jnp.concatenate(
        [leading * cosine - second * sine, second * cosine + leading * sine, unrotated], -1
    )


def body(
    tokens,
    lengths,
    slot_request,
    ln1_gain,
    ln1_bias,
    w_query,
    w_key,
    w_value,
    b_query,
    b_key,
    b_value,
    cache_keys,
    cache_values,
    w_out,
    ln2_gain,
    ln2_bias,
    w_gate,
    w_up,
    w_down,
):
    group_index = lax.axis_index("req")
    block_index = lax.axis_index("blk")
    count_req = tokens.shape[0]
    block_len = cache_keys.shape[1]
    col_count = w_query.shape[1]
    row_total = count_req * NEW
    column_start = block_index * col_count
    gathered = lax.all_gather(tokens, "req", axis=0, tiled=True)
    owned_slots = lax.dynamic_slice_in_dim(slot_request, group_index * count_req, count_req)
    inputs = jnp.take(gathered, owned_slots, axis=0).astype(jnp.float32)
    span_lengths = jnp.take(lengths, owned_slots)
    token_rows = inputs.reshape(row_total, D)
    normed = layer_norm(token_rows, ln1_gain, ln1_bias).astype(jnp.bfloat16)
    query_cols = (jnp.dot(normed, w_query, preferred_element_type=jnp.float32) + b_query).astype(
        jnp.bfloat16
    )
    key_cols = (jnp.dot(normed, w_key, preferred_element_type=jnp.float32) + b_key).astype(
        jnp.bfloat16
    )
    value_cols = (jnp.dot(normed, w_value, preferred_element_type=jnp.float32) + b_value).astype(
        jnp.bfloat16
    )
    query_raw, key_raw, value_raw = (
        lax.all_gather(query_cols, "blk", axis=1, tiled=True),
        lax.all_gather(key_cols, "blk", axis=1, tiled=True),
        lax.all_gather(value_cols, "blk", axis=1, tiled=True),
    )
    positions = span_lengths[:, None] + jnp.arange(NEW, dtype=jnp.int32)[None, :]
    head_shape = (count_req, NEW, HEADS, HEAD_DIM)
    queries = rotate(query_raw.astype(jnp.float32).reshape(head_shape), positions).astype(
        jnp.bfloat16
    )
    keys_new = rotate(key_raw.astype(jnp.float32).reshape(head_shape), positions).astype(
        jnp.bfloat16
    )
    values_new = value_raw.reshape(head_shape)
    new_keys_out = lax.dynamic_slice_in_dim(
        keys_new.reshape(count_req, NEW, D), column_start, col_count, 2
    )
    new_values_out = lax.dynamic_slice_in_dim(
        value_raw.reshape(count_req, NEW, D), column_start, col_count, 2
    )
    score_scale = HEAD_DIM ** (-0.5)
    key_heads = cache_keys.reshape(count_req, block_len, HEADS, HEAD_DIM)
    value_heads = cache_values.reshape(count_req, block_len, HEADS, HEAD_DIM)
    scores = (
        jnp.einsum("rthd,rphd->rthp", queries, key_heads, preferred_element_type=jnp.float32)
        * score_scale
    )
    places = block_index * block_len + jnp.arange(block_len, dtype=jnp.int32)
    visible = places[None, None, None, :] < span_lengths[:, None, None, None]
    peak_local = jnp.max(jnp.where(visible, scores, -1e30), -1)
    weights = jnp.where(visible, jnp.exp(scores - peak_local[..., None]), 0.0)
    total_local = jnp.sum(weights, -1)
    accum_local = jnp.einsum(
        "rthp,rphd->rthd",
        weights.astype(jnp.bfloat16),
        value_heads,
        preferred_element_type=jnp.float32,
    )
    fresh_scores = (
        jnp.einsum("rthd,rshd->rths", queries, keys_new, preferred_element_type=jnp.float32)
        * score_scale
    )
    causal = jnp.arange(NEW)[:, None, None] >= jnp.arange(NEW)[None, None, :]
    fresh_peak = jnp.max(jnp.where(causal, fresh_scores, -1e30), -1)
    fresh_weights = jnp.where(causal, jnp.exp(fresh_scores - fresh_peak[..., None]), 0.0)
    fresh_total = jnp.sum(fresh_weights, -1)
    fresh_accum = jnp.einsum(
        "rths,rshd->rthd",
        fresh_weights.astype(jnp.bfloat16),
        values_new,
        preferred_element_type=jnp.float32,
    )
    cache_peak = lax.pmax(peak_local, "blk")
    peak_all = jnp.maximum(cache_peak, fresh_peak)
    scale_local = jnp.exp(peak_local - peak_all)
    scale_new = jnp.exp(fresh_peak - peak_all)
    total_all, accum_all = lax.psum(
        (total_local * scale_local, accum_local * scale_local[..., None]), "blk"
    )
    numer = accum_all + fresh_accum * scale_new[..., None]
    denom = total_all + fresh_total * scale_new
    attended = (numer / denom[..., None]).astype(jnp.bfloat16).reshape(row_total, D)
    input_cols = lax.dynamic_slice_in_dim(token_rows, column_start, col_count, 1)
    residual = input_cols + jnp.dot(attended, w_out, preferred_element_type=jnp.float32)
    whole_rows = lax.all_gather(residual, "blk", axis=1, tiled=True)
    normed_two = layer_norm(whole_rows, ln2_gain, ln2_bias).astype(jnp.bfloat16)
    gate_proj = jnp.dot(normed_two, w_gate, preferred_element_type=jnp.float32)
    up_proj = jnp.dot(normed_two, w_up, preferred_element_type=jnp.float32)
    hidden = (jax.nn.silu(gate_proj) * up_proj).astype(jnp.bfloat16)
    down_cols = lax.psum_scatter(
        lax.dot_general(
            w_down, hidden, (((0,), (1,)), ((), ())), preferred_element_type=jnp.float32
        ),
        "blk",
        scatter_dimension=0,
        tiled=True,
    )
    layer_rows = (residual + down_cols.T).astype(jnp.bfloat16)
    return (layer_rows.reshape(count_req, NEW, col_count), new_keys_out, new_values_out)


def solution(mesh):
    return jax.shard_map(
        body,
        mesh=mesh,
        in_specs=(
            P("req", None, None),
            P(),
            P(),
            P(),
            P(),
            P(None, "blk"),
            P(None, "blk"),
            P(None, "blk"),
            P("blk"),
            P("blk"),
            P("blk"),
            P("req", "blk", None),
            P("req", "blk", None),
            P(None, "blk"),
            P(),
            P(),
            P(None, "blk"),
            P(None, "blk"),
            P("blk", None),
        ),
        out_specs=(P("req", None, "blk"), P("req", None, "blk"), P("req", None, "blk")),
        check_vma=False,
    )
```

profile of v0, /device:TPU:8, one launch (start us, length us, event | category | flops | bytes accessed | tf_op | source)
XLA Modules:
  0.0 900.7 jit_solution(16838919407700512123)
XLA Ops:
  7.3 0.8 compare_and_fusion
  8.1 13.9 %all_gather.15 = bf16[32,4,2048]{2,1,0:T(4,128)(2,1)S(1)} all-gather(bf16[8,4,2048]{2,1,0:T(4,128)(2,1)} %param.19), channel_id=1, replica_groups=mesh['blk'=64,'req'=4] {'req'}, dimensions={0}, use_global_device_ids=true | all-gather | bytes 655360 | tf_op jit(solution)/shard_map/all_gather | solution.py:62
  22.0 0.7 gather_fusion
  23.5 0.9 add_convert_fusion.2
  24.3 1.1 fusion.7
  25.5 53.3 %all_gather.17 = bf16[32,2048]{0,1:T(8,128)(2,1)S(1)} all-gather(bf16[32,32]{0,1:T(8,128)(2,1)S(1)} %copy.128), channel_id=1, replica_groups=mesh['blk'=64,'req'=4] {'blk'}, dimensions={1}, use_global_device_ids=true | all-gather | bytes 133120 | tf_op jit(solution)/shard_map/all_gather | solution.py:79
  79.8 49.3 %all_gather.16 = bf16[32,2048]{0,1:T(8,128)(2,1)S(1)} all-gather(bf16[32,32]{0,1:T(8,128)(2,1)S(1)} %copy.122), channel_id=1, replica_groups=mesh['blk'=64,'req'=4] {'blk'}, dimensions={1}, use_global_device_ids=true | all-gather | bytes 133120 | tf_op jit(solution)/shard_map/all_gather | solution.py:78
  129.9 0.6 gather_fusion.1
  131.6 0.9 multiply_subtract_fusion
  132.5 1.2 maximum_convert_fusion
  134.7 6.4 copy.126
  141.2 3.5 select_reduce_fusion
  144.6 248.7 %pmax.7 = f32[8,4,32]{1,2,0:T(8,128)S(1)} all-reduce(f32[8,4,32]{1,2,0:T(8,128)S(1)} %get-tuple-element.39), channel_id=1, replica_groups=mesh['blk'=64,'req'=4] {'blk'}, use_global_device_ids=true, to_apply=%region_3.4 | all-reduce | flops 1024 | bytes 8192 | tf_op jit(solution)/shard_map/pmax | solution.py:129
  393.4 0.7 fusion.10
  394.0 6.4 copy.127
  400.5 5.4 fusion
  406.3 246.5 %psum.15 = f32[8,4,32]{1,2,0:T(8,128)S(1)} all-reduce(f32[8,4,32]{1,2,0:T(8,128)S(1)} %get-tuple-element.23), channel_id=1, replica_groups=mesh['blk'=64,'req'=4] {'blk'}, use_global_device_ids=true, to_apply=%region_7.8 | all-reduce | flops 1024 | bytes 8192 | tf_op jit(solution)/shard_map/psum | solution.py:133
  653.3 47.0 %all_gather.18 = bf16[32,2048]{0,1:T(8,128)(2,1)S(1)} all-gather(bf16[32,32]{0,1:T(8,128)(2,1)S(1)} %copy.135), channel_id=1, replica_groups=mesh['blk'=64,'req'=4] {'blk'}, dimensions={1}, use_global_device_ids=true | all-gather | bytes 133120 | tf_op jit(solution)/shard_map/all_gather | solution.py:80
  700.9 1.7 fusion.5
  703.3 50.2 %all_gather.19 = f32[32,2048]{0,1:T(8,128)S(1)} all-gather(f32[32,32]{0,1:T(8,128)S(1)} %copy.142), channel_id=1, replica_groups=mesh['blk'=64,'req'=4] {'blk'}, dimensions={1}, use_global_device_ids=true | all-gather | bytes 266240 | tf_op jit(solution)/shard_map/all_gather | solution.py:141
  755.5 1.3 copy.146
  757.9 0.7 constant_dynamic-slice_fusion
  758.6 133.9 %reduce-scatter.4.cloned.1.call-done = f32[32,32]{1,0:T(8,128)} async-done(((f32[2048,32]{1,0:T(8,128)}), f32[32,32]{1,0:T(8,128)}) %reduce-scatter.4.cloned.1.call-update) | async-done | bytes 4112
  892.5 0.8 copy.147
  (89 shorter events, 10.4 us)
Async XLA Ops:
  7.2 747.8 %copy-start = (bf16[88,2048]{1,0:T(8,128)(2,1)S(1)}, bf16[88,2048]{1,0:T(8,128)(2,1)}, u32[]{:S(2)}) copy-start(bf16[88,2048]{1,0:T(8,128)(2,1)} %param.37) | copy-start | bytes 1081348
  7.2 72.4 %copy-start.4 = (bf16[2048,32]{0,1:T(8,128)(2,1)S(1)}, bf16[2048,32]{0,1:T(8,128)(2,1)}, u32[]{:S(2)}) copy-start(bf16[2048,32]{0,1:T(8,128)(2,1)} %param.24) | copy-start | bytes 393220
  7.2 72.4 %copy-start.9 = (f32[32]{0:T(128)S(1)}, f32[32]{0:T(128)}, u32[]{:S(2)}) copy-start(f32[32]{0:T(128)} %param.27) | copy-start | bytes 388
  7.2 693.7 %all-reduce.2.cloned.1.call-start = ((), (), s32[]{:S(2)}) async-start(), calls=%async_computation.1 | async-start | bytes 1048576 | tf_op jit(solution)/shard_map/psum | solution.py:133
  22.9 107.0 %copy-start.1 = (s32[32]{0:T(128)S(1)}, s32[32]{0:T(128)}, u32[]{:S(2)}) copy-start(s32[32]{0:T(128)} %param.20) | copy-start | bytes 388
  400.5 252.6 %copy-start.5 = (bf16[2048,32]{0,1:T(8,128)(2,1)S(1)}, bf16[2048,32]{0,1:T(8,128)(2,1)}, u32[]{:S(2)}) copy-start(bf16[2048,32]{0,1:T(8,128)(2,1)} %param.26) | copy-start | bytes 393220
  400.5 252.6 %copy-start.10 = (f32[32]{0:T(128)S(1)}, f32[32]{0:T(128)}, u32[]{:S(2)}) copy-start(f32[32]{0:T(128)} %param.29) | copy-start | bytes 388
  405.9 486.6 %reduce-scatter.4.cloned.1.call-start = ((), (), s32[]{:S(2)}) async-start(), calls=%async_computation.2 | async-start | bytes 1064960
  700.6 2.5 copy-start.6
  700.9 53.2 %copy-start.7 = (f32[2048]{0:T(1024)S(1)}, f32[2048]{0:T(1024)}, u32[]{:S(2)}) copy-start(f32[2048]{0:T(1024)} %param.34) | copy-start | bytes 24580
  700.9 53.2 %copy-start.8 = (f32[2048]{0:T(1024)S(1)}, f32[2048]{0:T(1024)}, u32[]{:S(2)}) copy-start(f32[2048]{0:T(1024)} %param.33) | copy-start | bytes 24580
  702.7 52.0 %copy-start.2 = (bf16[2048,88]{0,1:T(8,128)(2,1)S(1)}, bf16[2048,88]{0,1:T(8,128)(2,1)}, u32[]{:S(2)}) copy-start(bf16[2048,88]{0,1:T(8,128)(2,1)} %param.35) | copy-start | bytes 1081348
  702.7 52.3 %copy-start.3 = (bf16[2048,88]{0,1:T(8,128)(2,1)S(1)}, bf16[2048,88]{0,1:T(8,128)(2,1)}, u32[]{:S(2)}) copy-start(bf16[2048,88]{0,1:T(8,128)(2,1)} %param.36) | copy-start | bytes 1081348
Sparse Core Ops, SparseCore 0:
  406.0 177.1 all-reduce.1
  757.0 135.4 reduce-scatter.3
where the time goes:
time: 901 us
  blocking collectives  709 us (79%)
  waiting for transfers between devices  134 us (15%)
  local copies, waits for them, and re-layouts  22 us (2%)
  between operations  14.5 us (2%)
  matrix products  13.3 us (1%)
    pmax x1, blocking collectives, body(): cache_peak = lax.pmax(peak_local, 'blk')  249 us
    psum x1, blocking collectives, body(): lax.psum((total_local * scale_local, accum_local * scale_local[..., None]...  246 us
    unnamed x3, waiting for transfers between devices  134 us
    all_gather x1, blocking collectives, body(): lax.all_gather(key_cols, 'blk', axis=1, tiled=True)  53.3 us
    all_gather x1, blocking collectives, body(): whole_rows = lax.all_gather(residual, 'blk', axis=1, tiled=True)  50.2 us
    all_gather x1, blocking collectives, body(): lax.all_gather(query_cols, 'blk', axis=1, tiled=True)  49.3 us
    all_gather x1, blocking collectives, body(): lax.all_gather(value_cols, 'blk', axis=1, tiled=True)  47 us
  transfers between devices with their start and end apart: 2, of which 1 were waited for; matrix products, arithmetic and copies ran while one was open for 0% of the time, Pallas kernels for 0%

commit v1 on v0

--- a/solution.py
+++ b/solution.py
@@ -8,6 +8,14 @@
 HEAD_DIM = 64
 ROT = 16
 NEW = 4
+
+
+def gather_by_exchange(array, axis, dim):
+    size = lax.axis_size(axis)
+    repeats = [size if d == dim else 1 for d in range(array.ndim)]
+    return lax.all_to_all(
+        jnp.tile(array, repeats), axis, split_axis=dim, concat_axis=dim, tiled=True
+    )
 
 
 def layer_norm(values, norm_gain, norm_bias):
@@ -77,7 +85,7 @@
     query_raw, key_raw, value_raw = (
         lax.all_gather(query_cols, "blk", axis=1, tiled=True),
         lax.all_gather(key_cols, "blk", axis=1, tiled=True),
-        lax.all_gather(value_cols, "blk", axis=1, tiled=True),
+        gather_by_exchange(value_cols, "blk", 1),
     )
     positions = span_lengths[:, None] + jnp.arange(NEW, dtype=jnp.int32)[None, :]
     head_shape = (count_req, NEW, HEADS, HEAD_DIM)

time: 901 us -> 865 us (0.960)
  blocking collectives: 709 us -> 663 us
    all_gather x1 -> x0, blocking collectives: 47 us -> none  [body(): lax.all_gather(value_cols, 'blk', axis=1, tiled=True)]
  transfers between devices with their start and end apart: 2 -> 3, of which waited for: 1 -> 1; matrix products, arithmetic and copies ran while one was open for 0% -> 1% of each run, Pallas kernels for 0% -> 0%
where the time goes in v1:
time: 865 us; the launch traced here: 864 us
  blocking collectives  663 us (77%)
  waiting for transfers between devices  136 us (16%)
  local copies, waits for them, and re-layouts  23.9 us (3%)
  between operations  14.5 us (2%)
  matrix products  13.3 us (2%)
    psum x1, blocking collectives, body(): lax.psum((total_local * scale_local, accum_local * scale_local[..., None]...  251 us
    pmax x1, blocking collectives, body(): cache_peak = lax.pmax(peak_local, 'blk')  249 us
    unnamed x3, waiting for transfers between devices  136 us
    all_gather x1, blocking collectives, body(): lax.all_gather(key_cols, 'blk', axis=1, tiled=True)  53.3 us
    all_gather x1, blocking collectives, body(): lax.all_gather(query_cols, 'blk', axis=1, tiled=True)  49.3 us
    all_gather x1, blocking collectives, body(): whole_rows = lax.all_gather(residual, 'blk', axis=1, tiled=True)  47.1 us
    unnamed x32, local copies, waits for them, and re-layouts  17.4 us
  transfers between devices with their start and end apart: 3, of which 1 were waited for; matrix products, arithmetic and copies ran while one was open for 1% of the time, Pallas kernels for 0%

profile of v1, /device:TPU:8, one launch (start us, length us, event | category | flops | bytes accessed | tf_op | source)
XLA Modules:
  0.0 863.9 jit_solution(666217586148283406)
XLA Ops:
  7.3 0.8 compare_and_fusion
  8.1 13.9 %all_gather.12 = bf16[32,4,2048]{2,1,0:T(4,128)(2,1)S(1)} all-gather(bf16[8,4,2048]{2,1,0:T(4,128)(2,1)} %param.19), channel_id=1, replica_groups=mesh['blk'=64,'req'=4] {'req'}, dimensions={0}, use_global_device_ids=true | all-gather | bytes 655360 | tf_op jit(solution)/shard_map/all_gather | solution.py:70
  22.0 0.7 gather_fusion
  23.5 0.9 add_convert_fusion.2
  24.3 1.1 fusion.7
  25.5 53.3 %all_gather.14 = bf16[32,2048]{0,1:T(8,128)(2,1)S(1)} all-gather(bf16[32,32]{0,1:T(8,128)(2,1)S(1)} %copy.125), channel_id=1, replica_groups=mesh['blk'=64,'req'=4] {'blk'}, dimensions={1}, use_global_device_ids=true | all-gather | bytes 133120 | tf_op jit(solution)/shard_map/all_gather | solution.py:87
  79.8 49.3 %all_gather.13 = bf16[32,2048]{0,1:T(8,128)(2,1)S(1)} all-gather(bf16[32,32]{0,1:T(8,128)(2,1)S(1)} %copy.119), channel_id=1, replica_groups=mesh['blk'=64,'req'=4] {'blk'}, dimensions={1}, use_global_device_ids=true | all-gather | bytes 133120 | tf_op jit(solution)/shard_map/all_gather | solution.py:86
  131.6 0.9 multiply_subtract_fusion
  132.5 1.2 maximum_convert_fusion
  134.8 6.4 copy.123
  141.2 3.5 select_reduce_fusion
  144.7 248.7 %pmax.7 = f32[8,4,32]{1,2,0:T(8,128)S(1)} all-reduce(f32[8,4,32]{1,2,0:T(8,128)S(1)} %get-tuple-element.39), channel_id=1, replica_groups=mesh['blk'=64,'req'=4] {'blk'}, use_global_device_ids=true, to_apply=%region_3.4 | all-reduce | flops 1024 | bytes 8192 | tf_op jit(solution)/shard_map/pmax | solution.py:137
  393.4 0.7 fusion.10
  394.0 6.4 copy.124
  400.5 5.4 fusion
  406.2 1.1 reshape.247
  407.3 4.9 all-to-all-start
  412.9 251.1 %psum.15 = f32[8,4,32]{1,2,0:T(8,128)S(1)} all-reduce(f32[8,4,32]{1,2,0:T(8,128)S(1)} %get-tuple-element.23), channel_id=1, replica_groups=mesh['blk'=64,'req'=4] {'blk'}, use_global_device_ids=true, to_apply=%region_7.8 | all-reduce | flops 1024 | bytes 8192 | tf_op jit(solution)/shard_map/psum | solution.py:141
  664.8 1.7 fusion.5
  667.2 47.1 %all_gather.15 = f32[32,2048]{0,1:T(8,128)S(1)} all-gather(f32[32,32]{0,1:T(8,128)S(1)} %copy.138), channel_id=1, replica_groups=mesh['blk'=64,'req'=4] {'blk'}, dimensions={1}, use_global_device_ids=true | all-gather | bytes 266240 | tf_op jit(solution)/shard_map/all_gather | solution.py:149
  716.3 1.3 copy.142
  719.2 0.7 constant_dynamic-slice_fusion
  719.9 135.7 %reduce-scatter.4.cloned.1.call-done = f32[32,32]{1,0:T(8,128)} async-done(((f32[2048,32]{1,0:T(8,128)}), f32[32,32]{1,0:T(8,128)}) %reduce-scatter.4.cloned.1.call-update) | async-done | bytes 4112
  855.7 0.8 copy.143
  (92 shorter events, 11.8 us)
Async XLA Ops:
  7.2 708.7 %copy-start = (bf16[88,2048]{1,0:T(8,128)(2,1)S(1)}, bf16[88,2048]{1,0:T(8,128)(2,1)}, u32[]{:S(2)}) copy-start(bf16[88,2048]{1,0:T(8,128)(2,1)} %param.37) | copy-start | bytes 1081348
  7.2 72.4 %copy-start.4 = (bf16[2048,32]{0,1:T(8,128)(2,1)S(1)}, bf16[2048,32]{0,1:T(8,128)(2,1)}, u32[]{:S(2)}) copy-start(bf16[2048,32]{0,1:T(8,128)(2,1)} %param.24) | copy-start | bytes 393220
  7.2 72.4 %copy-start.9 = (f32[32]{0:T(128)S(1)}, f32[32]{0:T(128)}, u32[]{:S(2)}) copy-start(f32[32]{0:T(128)} %param.27) | copy-start | bytes 388
  7.2 657.6 %all-reduce.2.cloned.1.call-start = ((), (), s32[]{:S(2)}) async-start(), calls=%async_computation.2 | async-start | bytes 1048576 | tf_op jit(solution)/shard_map/psum | solution.py:141
  22.9 107.0 %copy-start.1 = (s32[32]{0:T(128)S(1)}, s32[32]{0:T(128)}, u32[]{:S(2)}) copy-start(s32[32]{0:T(128)} %param.20) | copy-start | bytes 388
  400.5 5.4 copy-start.5
  400.5 5.4 copy-start.10
  407.3 256.8 %all-to-all-start = ((bf16[64,2,512]{2,1,0:T(2,128)(2,1)}), bf16[64,2,512]{2,1,0:T(2,128)(2,1)S(1)}, u32[]{:S(2)}, u32[]{:S(2)}) async-start(bf16[64,2,512]{2,1,0:T(2,128)(2,1)} %reshape.247), calls=%async_computation | async-start | bytes 262144 | tf_op jit(solution)/shard_map/all_to_all | solution.py:16
  412.2 443.5 %reduce-scatter.4.cloned.1.call-start = ((), (), s32[]{:S(2)}) async-start(), calls=%async_computation.3 | async-start | bytes 1064960
  664.3 2.6 copy-start.6
  664.8 50.1 %copy-start.7 = (f32[2048]{0:T(1024)S(1)}, f32[2048]{0:T(1024)}, u32[]{:S(2)}) copy-start(f32[2048]{0:T(1024)} %param.34) | copy-start | bytes 24580
  664.8 50.1 %copy-start.8 = (f32[2048]{0:T(1024)S(1)}, f32[2048]{0:T(1024)}, u32[]{:S(2)}) copy-start(f32[2048]{0:T(1024)} %param.33) | copy-start | bytes 24580
  666.6 48.9 %copy-start.2 = (bf16[2048,88]{0,1:T(8,128)(2,1)S(1)}, bf16[2048,88]{0,1:T(8,128)(2,1)}, u32[]{:S(2)}) copy-start(bf16[2048,88]{0,1:T(8,128)(2,1)} %param.35) | copy-start | bytes 1081348
  666.6 49.2 %copy-start.3 = (bf16[2048,88]{0,1:T(8,128)(2,1)S(1)}, bf16[2048,88]{0,1:T(8,128)(2,1)}, u32[]{:S(2)}) copy-start(bf16[2048,88]{0,1:T(8,128)(2,1)} %param.36) | copy-start | bytes 1081348
Sparse Core Ops, SparseCore 0:
  406.0 176.8 all-reduce.1
  717.8 137.8 reduce-scatter.3
